TPU v7x, 32 devices: a whole 2x2x4 slice. The times are simulated.
32 devices in a mesh: wide: 4 (over y, core), narrow: 8 (over z, x).
Axes of the slice: x: 2, y: 2, z: 4, core: 2. Of those that a mesh axis runs over, the one named last changes fastest.
Arguments:
- tokens: bfloat16 [16384, 1024], P(('wide', 'narrow')), may hold values from -6 to 6
- cotangent: bfloat16 [16384, 1024], P(('wide', 'narrow')), may hold values from -6 to 6
- corpus_ids: int32 [8], P('wide'), may hold values from 0 to 7
- corpus_weights: float32 [8], replicated, may hold values from 0.3 to 3
- qkv_weight: bfloat16 [3, 1024, 1024], P(None, None, 'narrow'), may hold values from -0.1875 to 0.1875
- qkv_bias: float32 [3, 1024], P(None, 'narrow'), may hold values from -2 to 2
- out_weight: bfloat16 [1024, 1024], P('narrow'), may hold values from -0.75 to 0.75
- out_bias: float32 [1024], replicated, may hold values from -2 to 2
- up_weight: bfloat16 [1024, 4096], P(None, 'narrow'), may hold values from -0.1875 to 0.1875
- up_bias: float32 [4096], P('narrow'), may hold values from -3 to 3
- down_weight: bfloat16 [4096, 1024], P('narrow'), may hold values from -0.09375 to 0.09375
- down_bias: float32 [1024], replicated, may hold values from -2 to 2
- norm_gains: float32 [4, 1024], replicated, may hold values from 0.5 to 1.5
- norm_biases: float32 [4, 1024], replicated, may hold values from -2 to 2
Outputs:
- layer_out: bfloat16 [16384, 1024], P(('wide', 'narrow'))
- input_grad: bfloat16 [16384, 1024], P(('wide', 'narrow'))
- qkv_wgrad: float32 [3, 1024, 1024], P(None, None, 'narrow')
- qkv_bgrad: float32 [3, 1024], P(None, 'narrow')
- out_wgrad: float32 [1024, 1024], P('narrow')
- out_bgrad: float32 [1024], replicated
- up_wgrad: float32 [1024, 4096], P(None, 'narrow')
- up_bgrad: float32 [4096], P('narrow')
- down_wgrad: float32 [4096, 1024], P('narrow')
- down_bgrad: float32 [1024], replicated
- gain_grads: float32 [4, 1024], replicated
- bias_grads: float32 [4, 1024], replicated
All inputs are finite; a program needn't handle non-finite values.
Results may differ from a plain program's by a relative error of at most 0.023.
Values may be sent and summed in bfloat16 or wider, within the bound.
No kernel may reach another device: no remote copies, remote signals or barrier semaphores. Data moves between devices by JAX's collectives and lax.ppermute only.
A program may use at most 256 MiB of HBM per device.

v0:
```python
import math
import jax
import jax.numpy as jnp
from jax import lax
from jax.sharding import PartitionSpec as P

HEAD = 64
epsilon = 1e-05
root_half = 0.7071067811865476
gauss_norm = 0.3989422804014327
masked_score = -1e30


def norm_stats(vec_in):
    center = vec_in - jnp.mean(vec_in, axis=-1, keepdims=True)
    inverse = lax.rsqrt(jnp.mean(center * center, axis=-1, keepdims=True) + epsilon)
    return (center * inverse, inverse)


def norm_back(normed, inverse, gain_row, upstream):
    scaled = upstream * gain_row
    return inverse * (
        scaled
        - jnp.mean(scaled, axis=-1, keepdims=True)
        - normed * jnp.mean(scaled * normed, axis=-1, keepdims=True)
    )


def rotary_tables(length, head_size):
    half_size = head_size // 2
    inv_freq = jnp.exp(jnp.arange(half_size, dtype=jnp.float32) * (-math.log(10000.0) / half_size))
    angles = jnp.arange(length, dtype=jnp.float32)[:, None] * inv_freq[None, :]
    return (jnp.cos(angles), jnp.sin(angles))


def rotate(vectors, cos_table, sine_table):
    half_size = vectors.shape[-1] // 2
    front_half = vectors[..., :half_size]
    back_half = vectors[..., half_size:]
    cos_grid = cos_table[:, None, :]
    sin_grid = sine_table[:, None, :]
    return jnp.concatenate(
        [
            front_half * cos_grid - back_half * sin_grid,
            front_half * sin_grid + back_half * cos_grid,
        ],
        axis=-1,
    )


def rotate_back(vectors, cos_table, sine_table):
    half_size = vectors.shape[-1] // 2
    front_half = vectors[..., :half_size]
    back_half = vectors[..., half_size:]
    cos_grid = cos_table[:, None, :]
    sin_grid = sine_table[:, None, :]
    return jnp.concatenate(
        [
            front_half * cos_grid + back_half * sin_grid,
            back_half * cos_grid - front_half * sin_grid,
        ],
        axis=-1,
    )


def gelu_value(hidden):
    return 0.5 * hidden * (1.0 + lax.erf(hidden * root_half))


def gelu_slope(hidden):
    return (
        0.5 * (1.0 + lax.erf(hidden * root_half))
        + hidden * jnp.exp(-0.5 * hidden * hidden) * gauss_norm
    )


def project_qkv(gathered, qkv_weight, qkv_bias, cos_table, sine_table, seq_count, length):
    heads_here = qkv_weight.shape[2] // HEAD
    qkv_pre = (
        jnp.einsum("sd,tde->tse", gathered, qkv_weight, preferred_element_type=jnp.float32)
        + qkv_bias[:, None, :]
    )
    shaped = qkv_pre.reshape(3, seq_count, length, heads_here, HEAD)
    query = rotate(shaped[0], cos_table, sine_table).astype(jnp.bfloat16)
    key_rows = rotate(shaped[1], cos_table, sine_table).astype(jnp.bfloat16)
    values = shaped[2].astype(jnp.bfloat16)
    return (query, key_rows, values)


def block_scores(query, key_rows, block_start, block_rows):
    key_stop = block_start + block_rows
    query_block = query[:, block_start:key_stop]
    key_block = key_rows[:, :key_stop]
    scores = jnp.einsum(
        "bqhd,bkhd->bhqk", query_block, key_block, preferred_element_type=jnp.float32
    ) * (1.0 / math.sqrt(HEAD))
    query_pos = block_start + jnp.arange(block_rows)
    key_pos = jnp.arange(key_stop)
    allowed = key_pos[None, :] <= query_pos[:, None]
    return (jnp.where(allowed[None, None], scores, masked_score), query_block, key_block)


def attend_forward(query, key_rows, values, block_rows):
    length = query.shape[1]
    outputs = []
    totals = []
    for block_start in range(0, length, block_rows):
        key_stop = block_start + block_rows
        scores, query_block, key_block = block_scores(query, key_rows, block_start, block_rows)
        row_max = jnp.max(scores, axis=-1, keepdims=True)
        log_total = row_max + jnp.log(jnp.sum(jnp.exp(scores - row_max), axis=-1, keepdims=True))
        probs_low = jnp.exp(scores - log_total).astype(jnp.bfloat16)
        outputs.append(
            jnp.einsum(
                "bhqk,bkhd->bqhd",
                probs_low,
                values[:, :key_stop],
                preferred_element_type=jnp.float32,
            )
        )
        totals.append(log_total)
    return (jnp.concatenate(outputs, axis=1), totals)


def attend_backward(query, key_rows, values, attn_grad, totals, block_rows):
    length = query.shape[1]
    score_scale = 1.0 / math.sqrt(HEAD)
    keys_grad = jnp.zeros(key_rows.shape, jnp.float32)
    values_grad = jnp.zeros(values.shape, jnp.float32)
    query_grads = []
    for block_number, block_start in enumerate(range(0, length, block_rows)):
        key_stop = block_start + block_rows
        scores, query_block, key_block = block_scores(query, key_rows, block_start, block_rows)
        value_block = values[:, :key_stop]
        grad_block = attn_grad[:, block_start:key_stop]
        probs_full = jnp.exp(scores - totals[block_number])
        probs_low = probs_full.astype(jnp.bfloat16)
        probs_grad = jnp.einsum(
            "bqhd,bkhd->bhqk", grad_block, value_block, preferred_element_type=jnp.float32
        )
        row_dot = jnp.sum(probs_full * probs_grad, axis=-1, keepdims=True)
        scores_grad = (probs_full * (probs_grad - row_dot)).astype(jnp.bfloat16)
        query_grads.append(
            jnp.einsum(
                "bhqk,bkhd->bqhd", scores_grad, key_block, preferred_element_type=jnp.float32
            )
            * score_scale
        )
        pad_rows = ((0, 0), (0, length - key_stop), (0, 0), (0, 0))
        keys_grad = keys_grad + jnp.pad(
            jnp.einsum(
                "bhqk,bqhd->bkhd", scores_grad, query_block, preferred_element_type=jnp.float32
            )
            * score_scale,
            pad_rows,
        )
        values_grad = values_grad + jnp.pad(
            jnp.einsum(
                "bhqk,bqhd->bkhd", probs_low, grad_block, preferred_element_type=jnp.float32
            ),
            pad_rows,
        )
    return (jnp.concatenate(query_grads, axis=1), keys_grad, values_grad)


def shards(
    tokens,
    cotangent,
    corpus_ids,
    corpus_weights,
    qkv_weight,
    qkv_bias,
    out_weight,
    out_bias,
    up_weight,
    up_bias,
    down_weight,
    down_bias,
    norm_gains,
    norm_biases,
):
    shard_rows = tokens.shape[0]
    group_rows = shard_rows * lax.axis_size("narrow")
    seq_count = corpus_ids.shape[0]
    length = group_rows // seq_count
    block_rows = min(512, length)
    inner = qkv_weight.shape[2]
    first_row = lax.axis_index("narrow") * shard_rows
    cos_table, sine_table = rotary_tables(length, HEAD)
    layer_in = tokens.astype(jnp.float32)
    normed_first, inverse_first = norm_stats(layer_in)
    low_first = (normed_first * norm_gains[0] + norm_biases[0]).astype(jnp.bfloat16)
    gathered_first = lax.all_gather(low_first, "narrow", axis=0, tiled=True)
    query, key_rows, values = project_qkv(
        gathered_first, qkv_weight, qkv_bias, cos_table, sine_table, seq_count, length
    )
    attn_heads, totals = attend_forward(query, key_rows, values, block_rows)
    attn_low = attn_heads.reshape(group_rows, inner).astype(jnp.bfloat16)
    attn_rows = lax.all_to_all(attn_low, "narrow", 0, 1, tiled=True)
    out_full = lax.all_gather(out_weight, "narrow", axis=0, tiled=True)
    pre_attn = jnp.dot(attn_rows, out_full, preferred_element_type=jnp.float32) + out_bias
    normed_second, inverse_second = norm_stats(pre_attn)
    residual = layer_in + normed_second * norm_gains[1] + norm_biases[1]
    normed_third, inverse_third = norm_stats(residual)
    low_third = (normed_third * norm_gains[2] + norm_biases[2]).astype(jnp.bfloat16)
    gathered_third = lax.all_gather(low_third, "narrow", axis=0, tiled=True)
    hidden = jnp.dot(gathered_third, up_weight, preferred_element_type=jnp.float32) + up_bias
    act_low = gelu_value(hidden).astype(jnp.bfloat16)
    pre_mlp = (
        lax.psum_scatter(
            jnp.dot(act_low, down_weight, preferred_element_type=jnp.float32).astype(jnp.bfloat16),
            "narrow",
            scatter_dimension=0,
            tiled=True,
        ).astype(jnp.float32)
        + down_bias
    )
    normed_fourth, inverse_fourth = norm_stats(pre_mlp)
    final_sum = residual + normed_fourth * norm_gains[3] + norm_biases[3]
    layer_out = final_sum.astype(jnp.bfloat16)
    row_sequence = (first_row + jnp.arange(shard_rows, dtype=jnp.int32)) // length
    row_corpus = jnp.sum(
        jnp.where(
            row_sequence[:, None] == jnp.arange(seq_count, dtype=jnp.int32)[None, :],
            corpus_ids[None, :],
            0,
        ),
        axis=1,
    )
    row_weight = jnp.sum(
        jnp.where(
            row_corpus[:, None] == jnp.arange(corpus_weights.shape[0], dtype=jnp.int32)[None, :],
            corpus_weights[None, :],
            0.0,
        ),
        axis=1,
    )
    upstream = cotangent.astype(jnp.float32) * row_weight[:, None]
    mlp_grad = norm_back(normed_fourth, inverse_fourth, norm_gains[3], upstream).astype(
        jnp.bfloat16
    )
    mlp_full = lax.all_gather(mlp_grad, "narrow", axis=0, tiled=True)
    gathered_third = lax.all_gather(low_third, "narrow", axis=0, tiled=True)
    hidden = jnp.dot(gathered_third, up_weight, preferred_element_type=jnp.float32) + up_bias
    act_low = gelu_value(hidden).astype(jnp.bfloat16)
    down_wgrad = lax.dot_general(
        act_low, mlp_full, (((0,), (0,)), ((), ())), preferred_element_type=jnp.float32
    )
    act_grad = lax.dot_general(
        mlp_full, down_weight, (((1,), (1,)), ((), ())), preferred_element_type=jnp.float32
    )
    hidden_grad = (act_grad * gelu_slope(hidden)).astype(jnp.bfloat16)
    up_bgrad = jnp.sum(hidden_grad.astype(jnp.float32), axis=0)
    up_wgrad = lax.dot_general(
        gathered_third, hidden_grad, (((0,), (0,)), ((), ())), preferred_element_type=jnp.float32
    )
    rows_here = hidden_grad
    third_grad = lax.psum_scatter(
        lax.dot_general(
            rows_here, up_weight, (((1,), (1,)), ((), ())), preferred_element_type=jnp.float32
        ).astype(jnp.bfloat16),
        "narrow",
        scatter_dimension=0,
        tiled=True,
    ).astype(jnp.float32)
    residual_grad = upstream + norm_back(normed_third, inverse_third, norm_gains[2], third_grad)
    branch_grad = norm_back(normed_second, inverse_second, norm_gains[1], residual_grad).astype(
        jnp.bfloat16
    )
    gathered_first = lax.all_gather(low_first, "narrow", axis=0, tiled=True)
    query, key_rows, values = project_qkv(
        gathered_first, qkv_weight, qkv_bias, cos_table, sine_table, seq_count, length
    )
    attn_grad_rows = lax.dot_general(
        branch_grad, out_full, (((1,), (1,)), ((), ())), preferred_element_type=jnp.float32
    ).astype(jnp.bfloat16)
    attn_grad = lax.all_to_all(attn_grad_rows, "narrow", 1, 0, tiled=True)
    attn_grad = attn_grad.reshape(query.shape)
    query_grad, keys_grad, values_grad = attend_backward(
        query, key_rows, values, attn_grad, totals, block_rows
    )
    out_wgrad_rows = lax.dot_general(
        attn_rows, branch_grad, (((0,), (0,)), ((), ())), preferred_element_type=jnp.float32
    )
    out_wgrad = lax.psum_scatter(
        out_wgrad_rows.astype(jnp.bfloat16), "narrow", scatter_dimension=0, tiled=True
    )
    qkv_grad = jnp.stack(
        [
            rotate_back(query_grad, cos_table, sine_table),
            rotate_back(keys_grad, cos_table, sine_table),
            values_grad,
        ]
    )
    qkv_grad = qkv_grad.reshape(3, group_rows, inner).astype(jnp.bfloat16)
    qkv_bgrad = jnp.sum(qkv_grad.astype(jnp.float32), axis=1)
    qkv_wgrad = jnp.einsum(
        "sd,tse->tde", gathered_first, qkv_grad, preferred_element_type=jnp.float32
    )
    rows_here = qkv_grad
    first_grad = lax.psum_scatter(
        jnp.einsum("tse,tde->sd", rows_here, qkv_weight, preferred_element_type=jnp.float32).astype(
            jnp.bfloat16
        ),
        "narrow",
        scatter_dimension=0,
        tiled=True,
    ).astype(jnp.float32)
    input_grad = (
        residual_grad + norm_back(normed_first, inverse_first, norm_gains[0], first_grad)
    ).astype(jnp.bfloat16)
    gain_local = jnp.stack(
        [
            jnp.sum(first_grad * normed_first, axis=0),
            jnp.sum(residual_grad * normed_second, axis=0),
            jnp.sum(third_grad * normed_third, axis=0),
            jnp.sum(upstream * normed_fourth, axis=0),
        ]
    )
    bias_local = jnp.stack(
        [
            jnp.sum(first_grad, axis=0),
            jnp.sum(residual_grad, axis=0),
            jnp.sum(third_grad, axis=0),
            jnp.sum(upstream, axis=0),
        ]
    )
    out_blocal = jnp.sum(branch_grad.astype(jnp.float32), axis=0)
    down_blocal = jnp.sum(mlp_grad.astype(jnp.float32), axis=0)
    weight_sums = (
        lax.psum(qkv_wgrad.astype(jnp.bfloat16), "wide").astype(jnp.float32),
        lax.psum(qkv_bgrad.astype(jnp.bfloat16), "wide").astype(jnp.float32),
        lax.psum(out_wgrad, "wide").astype(jnp.float32),
        lax.psum(up_wgrad.astype(jnp.bfloat16), "wide").astype(jnp.float32),
        lax.psum(up_bgrad.astype(jnp.bfloat16), "wide").astype(jnp.float32),
        lax.psum(down_wgrad.astype(jnp.bfloat16), "wide").astype(jnp.float32),
    )
    small_sums = lax.psum((gain_local, bias_local, out_blocal, down_blocal), ("wide", "narrow"))
    return (
        layer_out,
        input_grad,
        weight_sums[0],
        weight_sums[1],
        weight_sums[2],
        small_sums[2],
        weight_sums[3],
        weight_sums[4],
        weight_sums[5],
        small_sums[3],
        small_sums[0],
        small_sums[1],
    )


def solution(mesh):
    return jax.shard_map(
        shards,
        mesh=mesh,
        in_specs=(
            P(("wide", "narrow"), None),
            P(("wide", "narrow"), None),
            P("wide"),
            P(),
            P(None, None, "narrow"),
            P(None, "narrow"),
            P("narrow", None),
            P(),
            P(None, "narrow"),
            P("narrow"),
            P("narrow", None),
            P(),
            P(),
            P(),
        ),
        out_specs=(
            P(("wide", "narrow"), None),
            P(("wide", "narrow"), None),
            P(None, None, "narrow"),
            P(None, "narrow"),
            P("narrow", None),
            P(),
            P(None, "narrow"),
            P("narrow"),
            P("narrow", None),
            P(),
            P(),
            P(),
        ),
        check_vma=False,
    )
```

profile of v0, /device:TPU:0, one launch (start us, length us, event | category | flops | bytes accessed | tf_op | source)
XLA Modules:
  0.0 1326.1 jit_solution(15998260063616890509)
XLA Ops:
  19.9 122.4 %all-gather.5.cloned.1.call-done = bf16[4096,1024]{1,0:T(8,128)(2,1)} async-done(((bf16[512,1024]{1,0:T(8,128)(2,1)}), bf16[4096,1024]{1,0:T(8,128)(2,1)}) %all-gather.5.cloned.1.call-update) | async-done | bytes 8388624 | tf_op jit(solution)/shard_map/all_gather | solution.py:193
  142.3 7.1 add_bitcast_fusion
  157.9 5.9 copy.105
  169.3 5.7 reshape.336
  175.0 9.7 fusion.130
  184.7 6.4 copy.154
  191.2 6.4 copy.155
  197.6 10.1 fusion.129
  207.7 6.4 copy.156
  214.1 6.4 copy.157
  264.5 25.4 %all-to-all-done = bf16[8,512,128]{1,2,0:T(8,128)(2,1)S(1)} async-done(((bf16[8,512,128]{1,2,0:T(8,128)(2,1)}), bf16[8,512,128]{1,2,0:T(8,128)(2,1)S(1)}, u32[]{:S(2)}, u32[]{:S(2)}) %all-to-all-start) | async-done | bytes 1048608 | tf_op jit(solution)/shard_map/all_to_all | solution.py:199
  299.3 123.4 %all-gather.9.cloned.1.call-done = bf16[4096,1024]{1,0:T(8,128)(2,1)} async-done(((bf16[512,1024]{1,0:T(8,128)(2,1)}), bf16[4096,1024]{1,0:T(8,128)(2,1)}) %all-gather.9.cloned.1.call-update) | async-done | bytes 8388624 | tf_op jit(solution)/shard_map/all_gather | solution.py:206
  422.7 10.0 multiply_convert_fusion.3
  434.7 6.7 convolution_convert_fusion.1
  442.1 145.0 %reduce-scatter.5.cloned.1.call-done = bf16[512,1024]{1,0:T(8,128)(2,1)} async-done(((bf16[4096,1024]{1,0:T(8,128)(2,1)}), bf16[512,1024]{1,0:T(8,128)(2,1)}) %reduce-scatter.5.cloned.1.call-update) | async-done | bytes 1048592 | tf_op jit(solution)/shard_map/reduce_scatter | solution.py:210
  596.4 123.7 %all-gather.11.cloned.1.call-done = bf16[4096,1024]{1,0:T(8,128)(2,1)} async-done(((bf16[512,1024]{1,0:T(8,128)(2,1)}), bf16[4096,1024]{1,0:T(8,128)(2,1)}) %all-gather.11.cloned.1.call-update) | async-done | bytes 8388624 | tf_op jit(solution)/shard_map/all_gather | solution.py:242
  720.1 12.4 fusion.134
  734.5 7.3 convolution_convert_fusion
  741.8 145.8 %reduce-scatter.7.cloned.1.call-done = bf16[512,1024]{1,0:T(8,128)(2,1)} async-done(((bf16[4096,1024]{1,0:T(8,128)(2,1)}), bf16[512,1024]{1,0:T(8,128)(2,1)}) %reduce-scatter.7.cloned.1.call-update) | async-done | bytes 1048592 | tf_op jit(solution)/shard_map/reduce_scatter | solution.py:258
  904.2 10.3 convolution_convert_fusion.3
  914.4 8.2 convolution_convert_fusion.4
  965.5 7.4 multiply_reduce_fusion.1
  972.9 10.6 multiply_convert_fusion.1
  988.7 11.6 multiply_reduce_fusion
  1000.4 7.5 fusion.29
  1014.2 12.4 multiply_convert_fusion
  1047.2 6.9 fusion.60
  1054.1 8.8 bitcast_convert_fusion
  1065.4 6.5 all-reduce.7
  1073.1 48.5 %all-reduce.11.cloned.1.call-done = (bf16[3,1024,128]{1,2,0:T(8,128)(2,1)}, bf16[128,1024]{1,0:T(8,128)(2,1)}, bf16[1024,512]{1,0:T(8,128)(2,1)}, bf16[512,1024]{1,0:T(8,128)(2,1)}) async-done(((bf16[3,1024,128]{1,2,0:T(8,128)(2,1)}, bf16[128,1024]{1,0:T(8,128)(2,1)}, bf16[1024,512]{1,0:T(8,128)(2,1)}, bf16[512,1024]{1,0:T(8,128)(2,1)}), (bf16[3,1024,128]{1,2,0:T(8,128)(2,1)}, bf16[128,1024]{1,0:T(8,128)(2,1)}, ...) | async-done | bytes 3145744 | tf_op jit(solution)/shard_map/psum | solution.py:331
  1130.6 142.2 %reduce-scatter.9.cloned.1.call-done = bf16[512,1024]{1,0:T(8,128)(2,1)} async-done(((bf16[4096,1024]{1,0:T(8,128)(2,1)}), bf16[512,1024]{1,0:T(8,128)(2,1)}) %reduce-scatter.9.cloned.1.call-update) | async-done | bytes 1048592 | tf_op jit(solution)/shard_map/reduce_scatter | solution.py:301
  1275.2 40.3 %all-reduce.6 = (f32[1024]{0:T(1024)}, f32[1024]{0:T(1024)}, f32[4,1024]{1,0:T(4,128)}, f32[4,1024]{1,0:T(4,128)}) all-reduce(f32[1024]{0:T(1024)S(1)} %copy-done.74, f32[1024]{0:T(1024)S(1)} %copy-done.70, f32[4,1024]{1,0:T(4,128)S(1)} %pad_maximum_fusion.9, ...), channel_id=1, replica_groups=mesh['wide'=4,'narrow'=8] {'wide','narrow'}, use_global_device_ids=true, to_apply=%region_39.40 | all-reduce | flops 10240 | bytes 81920 | tf_op jit(solution)/shard_map/psum | solution.py:338
  (334 shorter events, 203.2 us)
Async XLA Ops:
  7.2 415.5 %copy-start = (bf16[1024,512]{1,0:T(8,128)(2,1)S(1)}, bf16[1024,512]{1,0:T(8,128)(2,1)}, u32[]{:S(2)}) copy-start(bf16[1024,512]{1,0:T(8,128)(2,1)} %param.22) | copy-start | bytes 3145732
  7.2 135.1 %copy-start.82 = (f32[3,128]{1,0:T(4,128)S(1)}, f32[3,128]{1,0:T(4,128)}, u32[]{:S(2)}) copy-start(f32[3,128]{1,0:T(4,128)} %param.19) | copy-start | bytes 4612
  7.2 135.1 %all-gather.5.cloned.1.call-start = ((), (), s32[]{:S(2)}) async-start(), calls=%async_computation.6 | async-start | bytes 9437184 | tf_op jit(solution)/shard_map/all_gather | solution.py:193
  14.9 249.6 %all-gather.7.cloned.1.call-start = ((), (), s32[]{:S(2)}) async-start(), calls=%async_computation.7 | async-start | bytes 2359296 | tf_op jit(solution)/shard_map/all_gather | solution.py:200
  16.9 219.8 %copy-start.21 = (pred[512,1024]{1,0:T(8,128)(4,1)}, pred[512,1024]{1,0:T(8,128)(4,1)S(1)}, u32[]{:S(2)}) copy-start(pred[512,1024]{1,0:T(8,128)(4,1)S(1)} %iota_compare_fusion.2) | copy-start | bytes 1572868
  19.2 220.7 %copy-start.14 = (pred[512,1536]{1,0:T(8,128)(4,1)}, pred[512,1536]{1,0:T(8,128)(4,1)S(1)}, u32[]{:S(2)}) copy-start(pred[512,1536]{1,0:T(8,128)(4,1)S(1)} %iota_compare_fusion.1) | copy-start | bytes 2359300
  19.9 233.1 %copy-start.10 = (pred[512,2048]{1,0:T(8,128)(4,1)}, pred[512,2048]{1,0:T(8,128)(4,1)S(1)}, u32[]{:S(2)}) copy-start(pred[512,2048]{1,0:T(8,128)(4,1)S(1)} %iota_compare_fusion) | copy-start | bytes 3145732
  257.8 33.1 %copy-start.61 = (f32[1024]{0:T(1024)S(1)}, f32[1024]{0:T(1024)}, u32[]{:S(2)}) copy-start(f32[1024]{0:T(1024)} %param.21) | copy-start | bytes 12292
  260.9 29.0 %all-to-all-start = ((bf16[8,512,128]{1,2,0:T(8,128)(2,1)}), bf16[8,512,128]{1,2,0:T(8,128)(2,1)S(1)}, u32[]{:S(2)}, u32[]{:S(2)}) async-start(bf16[8,512,128]{1,2,0:T(8,128)(2,1)} %copy.117), calls=%async_computation | async-start | bytes 2097152 | tf_op jit(solution)/shard_map/all_to_all | solution.py:199
  264.5 158.2 %all-gather.9.cloned.1.call-start = ((), (), s32[]{:S(2)}) async-start(), calls=%async_computation.8 | async-start | bytes 9437184 | tf_op jit(solution)/shard_map/all_gather | solution.py:206
  296.5 126.1 %copy-start.83 = (f32[512]{0:T(512)S(1)}, f32[512]{0:T(512)}, u32[]{:S(2)}) copy-start(f32[512]{0:T(512)} %param.23) | copy-start | bytes 6148
  299.3 287.9 %reduce-scatter.5.cloned.1.call-start = ((), (), s32[]{:S(2)}) async-start(), calls=%async_computation.9 | async-start | bytes 9437184 | tf_op jit(solution)/shard_map/reduce_scatter | solution.py:210
  441.3 145.8 %copy-start.62 = (f32[1024]{0:T(1024)S(1)}, f32[1024]{0:T(1024)}, u32[]{:S(2)}) copy-start(f32[1024]{0:T(1024)} %param.25) | copy-start | bytes 12292
  441.3 278.7 %all-gather.11.cloned.1.call-start = ((), (), s32[]{:S(2)}) async-start(), calls=%async_computation.10 | async-start | bytes 9437184 | tf_op jit(solution)/shard_map/all_gather | solution.py:242
  596.4 291.3 %reduce-scatter.7.cloned.1.call-start = ((), (), s32[]{:S(2)}) async-start(), calls=%async_computation.11 | async-start | bytes 9437184 | tf_op jit(solution)/shard_map/reduce_scatter | solution.py:258
  741.8 145.8 %copy-start.13 = (bf16[512,1024]{1,0:T(8,128)(2,1)S(1)}, bf16[512,1024]{1,0:T(8,128)(2,1)}, u32[]{:S(2)}) copy-start(bf16[512,1024]{1,0:T(8,128)(2,1)} %reduce-scatter.5.cloned.1.call-done) | copy-start | bytes 3145732
  900.4 29.6 %all-to-all-start.1 = ((bf16[512,8,128]{0,2,1:T(8,128)(2,1)}), bf16[512,8,128]{0,2,1:T(8,128)(2,1)S(1)}, u32[]{:S(2)}, u32[]{:S(2)}) async-start(bf16[512,8,128]{0,2,1:T(8,128)(2,1)} %bitcast.16), calls=%async_computation.3 | async-start | bytes 2097152 | tf_op jit(solution)/shard_map/all_to_all | solution.py:277
  904.1 150.0 %reduce-scatter.11.cloned.1.call-start = ((), (), s32[]{:S(2)}) async-start(), calls=%async_computation.13 | async-start | bytes 2359296 | tf_op jit(solution)/shard_map/reduce_scatter | solution.py:285
  925.3 196.3 %all-reduce.11.cloned.1.call-start = ((), (), s32[]{:S(2)}) async-start(), calls=%async_computation.14 | async-start | bytes 6291456 | tf_op jit(solution)/shard_map/psum | solution.py:331
  1054.1 218.7 %reduce-scatter.9.cloned.1.call-start = ((), (), s32[]{:S(2)}) async-start(), calls=%async_computation.12 | async-start | bytes 9437184 | tf_op jit(solution)/shard_map/reduce_scatter | solution.py:301
  1123.4 149.3 %copy-start.9 = (bf16[512,1024]{1,0:T(8,128)(2,1)S(1)}, bf16[512,1024]{1,0:T(8,128)(2,1)}, u32[]{:S(2)}) copy-start(bf16[512,1024]{1,0:T(8,128)(2,1)} %param.14) | copy-start | bytes 3145732
  1123.4 149.3 %copy-start.64 = (f32[1,1024]{1,0:T(1,128)S(1)}, f32[1,1024]{1,0:T(1,128)}, u32[]{:S(2)}) copy-start(f32[1,1024]{1,0:T(1,128)} %copy-done.63) | copy-start | bytes 12292
  1123.4 149.3 %copy-start.66 = (f32[512]{0:T(512)S(1)}, f32[512]{0:T(512)}, u32[]{:S(2)}) copy-start(f32[512]{0:T(512)} %copy-done.65) | copy-start | bytes 6148
  1123.4 149.3 %copy-start.68 = (f32[512]{0:T(512)S(1)}, f32[512]{0:T(512)}, u32[]{:S(2)}) copy-start(f32[512]{0:T(512)} %copy-done.67) | copy-start | bytes 6148
  1126.1 148.9 %copy-start.72 = (f32[1024]{0:T(1024)S(1)}, f32[1024]{0:T(1024)}, u32[]{:S(2)}) copy-start(f32[1024]{0:T(1024)} %get-tuple-element.64) | copy-start | bytes 12292
  1126.1 149.0 %copy-start.73 = (f32[1024]{0:T(1024)S(1)}, f32[1024]{0:T(1024)}, u32[]{:S(2)}) copy-start(f32[1024]{0:T(1024)} %get-tuple-element.60) | copy-start | bytes 12292
  1126.1 149.0 %copy-start.76 = (f32[1024]{0:T(1024)S(1)}, f32[1024]{0:T(1024)}, u32[]{:S(2)}) copy-start(f32[1024]{0:T(1024)} %get-tuple-element.62) | copy-start | bytes 12292
  1126.1 149.0 %copy-start.71 = (f32[1024]{0:T(1024)S(1)}, f32[1024]{0:T(1024)}, u32[]{:S(2)}) copy-start(f32[1024]{0:T(1024)} %get-tuple-element.73) | copy-start | bytes 12292
  1126.1 149.0 %copy-start.75 = (f32[1024]{0:T(1024)S(1)}, f32[1024]{0:T(1024)}, u32[]{:S(2)}) copy-start(f32[1024]{0:T(1024)} %get-tuple-element.75) | copy-start | bytes 12292
  1126.1 149.0 %copy-start.70 = (f32[1024]{0:T(1024)S(1)}, f32[1024]{0:T(1024)}, u32[]{:S(2)}) copy-start(f32[1024]{0:T(1024)} %get-tuple-element.86) | copy-start | bytes 12292
  1126.1 149.0 %copy-start.74 = (f32[1024]{0:T(1024)S(1)}, f32[1024]{0:T(1024)}, u32[]{:S(2)}) copy-start(f32[1024]{0:T(1024)} %get-tuple-element.88) | copy-start | bytes 12292
  1129.0 190.1 %copy-start.1 = (bf16[1024,512]{1,0:T(8,128)(2,1)S(1)}, bf16[1024,512]{1,0:T(8,128)(2,1)}, u32[]{:S(2)}) copy-start(bf16[1024,512]{1,0:T(8,128)(2,1)} %param.22) | copy-start | bytes 3145732
  (75 other events, 417.4 us)
Sparse Core Ops, SparseCore 0:
  15.0 127.2 all-gather.4
  144.4 47.2 all-gather.6
  299.4 123.2 all-gather.8
  441.5 145.6 reduce-scatter.4
  596.5 123.5 all-gather.10
  742.0 145.6 reduce-scatter.6
  925.4 69.7 reduce-scatter.10
  1054.2 67.3 all-reduce.10
  1125.2 147.5 reduce-scatter.8
where the time goes:
time: 1340 us; the launch traced here: 1330 us
  waiting for transfers between devices  881 us (66%)
  matrix products  168 us (13%)
  local copies, waits for them, and re-layouts  110 us (8%)
  other arithmetic  96.1 us (7%)
  blocking collectives  46.8 us (3%)
  between operations  15.4 us (1%)
    reduce_scatter x1, waiting for transfers between devices, shards(): lax.psum_scatter(lax.dot_general(rows_here, up_weight, (((1,), (1,)), (()...  146 us
    reduce_scatter x1, waiting for transfers between devices, shards(): lax.psum_scatter(jnp.dot(act_low, down_weight, preferred_element_type=jnp...  145 us
    reduce_scatter x1, waiting for transfers between devices, shards(): lax.psum_scatter(jnp.einsum('tse,tde->sd', rows_here, qkv_weight, preferr...  142 us
    all_gather x1, waiting for transfers between devices, shards(): mlp_full = lax.all_gather(mlp_grad, 'narrow', axis=0, tiled=True)  124 us
    all_gather x1, waiting for transfers between devices, shards(): gathered_third = lax.all_gather(low_third, 'narrow', axis=0, tiled=True)  123 us
    all_gather x1, waiting for transfers between devices, shards(): gathered_first = lax.all_gather(low_first, 'narrow', axis=0, tiled=True)  122 us
    psum x1, waiting for transfers between devices, shards(): lax.psum(qkv_wgrad.astype(jnp.bfloat16), 'wide').astype(jnp.float32)  48.5 us
    unnamed x199, local copies, waits for them, and re-layouts  42.6 us
  transfers between devices with their start and end apart: 11, of which 9 were waited for; matrix products, arithmetic and copies ran while one was open for 21% of the time, Pallas kernels for 0%

commit v1 on v0

--- a/solution.py
+++ b/solution.py
@@ -1,3 +1,4 @@
+import functools
 import math
 import jax
 import jax.numpy as jnp
@@ -9,6 +10,28 @@
 root_half = 0.7071067811865476
 gauss_norm = 0.3989422804014327
 masked_score = -1e30
+
+
+def _watch_tiles(sheet, mesh_dim):
+    h_now, met_up, a_next = (lax.axis_size(mesh_dim), lax.axis_index(mesh_dim), sheet.shape[0])
+    z, earlier = (sheet, 1)
+    while earlier < h_now:
+        z = jnp.concatenate(
+            [
+                z,
+                lax.ppermute(
+                    z,
+                    axis_name=mesh_dim,
+                    perm=list(map(lambda idx: (idx, (idx - earlier) % h_now), range(h_now))),
+                ),
+            ],
+            axis=0,
+        )
+        earlier = 2 * earlier
+    return jnp.roll(z, shift=met_up * a_next, axis=0)
+
+
+change_yards = functools.partial(_watch_tiles, mesh_dim="narrow")
 
 
 def norm_stats(vec_in):
@@ -190,7 +213,7 @@
     layer_in = tokens.astype(jnp.float32)
     normed_first, inverse_first = norm_stats(layer_in)
     low_first = (normed_first * norm_gains[0] + norm_biases[0]).astype(jnp.bfloat16)
-    gathered_first = lax.all_gather(low_first, "narrow", axis=0, tiled=True)
+    gathered_first = change_yards(low_first)
     query, key_rows, values = project_qkv(
         gathered_first, qkv_weight, qkv_bias, cos_table, sine_table, seq_count, length
     )

time: 1340 us -> 1670 us (1.25)
  waiting for transfers between devices: 881 us -> 1070 us
  local copies, waits for them, and re-layouts: 110 us -> 206 us
  matrix products: 168 us -> 202 us
    ppermute x0 -> x3, waiting for transfers between devices: none -> 347 us  [_watch_tiles(): lax.ppermute(z, axis_name=mesh_dim, perm=list(map(lambda idx: (idx, (idx...]
    all_gather x1, waiting for transfers between devices: 122 us -> 0.01 us  [shards(): gathered_first = lax.all_gather(low_first, 'narrow', axis=0, tiled=True)]
    unnamed x199 -> x223, local copies, waits for them, and re-layouts: 42.6 us -> 84 us
    reduce_scatter x1, waiting for transfers between devices: 146 us -> 114 us  [shards(): lax.psum_scatter(lax.dot_general(rows_here, up_weight, (((1,), (1,)), (()...]
    dot_general x4 -> x8, matrix products: 8.36 us -> 33.9 us  [block_scores(): jnp.einsum('bqhd,bkhd->bhqk', query_block, key_block, preferred_element_t...]
    slice x2 -> x4, local copies, waits for them, and re-layouts: 19.8 us -> 39.5 us  [rotate(): front_half = vectors[..., :half_size]]
  transfers between devices with their start and end apart: 11 -> 14, of which waited for: 9 -> 11; matrix products, arithmetic and copies ran while one was open for 21% -> 25% of each run, Pallas kernels for 0% -> 0%
where the time goes in v1:
time: 1670 us; the launch traced here: 1660 us
  waiting for transfers between devices  1070 us (64%)
  local copies, waits for them, and re-layouts  206 us (12%)
  matrix products  202 us (12%)
  other arithmetic  101 us (6%)
  blocking collectives  46.8 us (3%)
    ppermute x3, waiting for transfers between devices, _watch_tiles(): lax.ppermute(z, axis_name=mesh_dim, perm=list(map(lambda idx: (idx, (idx...  347 us
    reduce_scatter x1, waiting for transfers between devices, shards(): lax.psum_scatter(jnp.dot(act_low, down_weight, preferred_element_type=jnp...  145 us
    reduce_scatter x1, waiting for transfers between devices, shards(): lax.psum_scatter(jnp.einsum('tse,tde->sd', rows_here, qkv_weight, preferr...  142 us
    all_gather x1, waiting for transfers between devices, shards(): mlp_full = lax.all_gather(mlp_grad, 'narrow', axis=0, tiled=True)  124 us
    all_gather x1, waiting for transfers between devices, shards(): gathered_third = lax.all_gather(low_third, 'narrow', axis=0, tiled=True)  123 us
    reduce_scatter x1, waiting for transfers between devices, shards(): lax.psum_scatter(lax.dot_general(rows_here, up_weight, (((1,), (1,)), (()...  114 us
    unnamed x223, local copies, waits for them, and re-layouts  84 us
    psum x1, waiting for transfers between devices, shards(): lax.psum(qkv_wgrad.astype(jnp.bfloat16), 'wide').astype(jnp.float32)  48.6 us
  transfers between devices with their start and end apart: 14, of which 11 were waited for; matrix products, arithmetic and copies ran while one was open for 25% of the time, Pallas kernels for 0%

profile of v1, /device:TPU:0, one launch (start us, length us, event | category | flops | bytes accessed | tf_op | source)
XLA Modules:
  0.0 1661.3 jit_solution(12252595174355461433)
XLA Ops:
  22.5 40.6 %collective-permute-done = bf16[512,1024]{1,0:T(8,128)(2,1)S(1)} collective-permute-done((bf16[512,1024]{1,0:T(8,128)(2,1)}, bf16[512,1024]{1,0:T(8,128)(2,1)S(1)}, u32[]{:S(2)}, u32[]{:S(2)}) %collective-permute-start) | collective-permute-done | bytes 1048608 | tf_op jit(solution)/shard_map/ppermute | solution.py:22
  65.1 58.8 %collective-permute-done.1 = bf16[1024,1024]{1,0:T(8,128)(2,1)S(1)} collective-permute-done((bf16[1024,1024]{1,0:T(8,128)(2,1)S(1)}, bf16[1024,1024]{1,0:T(8,128)(2,1)S(1)}, u32[]{:S(2)}, u32[]{:S(2)}) %collective-permute-start.1) | collective-permute-done | bytes 2097184 | tf_op jit(solution)/shard_map/ppermute | solution.py:22
  138.4 247.3 %collective-permute-done.2 = bf16[2048,1024]{1,0:T(8,128)(2,1)} collective-permute-done((bf16[2048,1024]{1,0:T(8,128)(2,1)}, bf16[2048,1024]{1,0:T(8,128)(2,1)}, u32[]{:S(2)}, u32[]{:S(2)}) %collective-permute-start.2) | collective-permute-done | bytes 4194336 | tf_op jit(solution)/shard_map/ppermute | solution.py:22
  398.8 7.0 add_bitcast_fusion.1
  427.2 9.9 fusion.205
  448.6 10.1 fusion.204
  471.5 7.1 add_bitcast_fusion
  493.8 9.7 fusion.203
  516.4 9.9 fusion.202
  585.7 25.0 %all-to-all-done = bf16[8,512,128]{1,2,0:T(8,128)(2,1)S(1)} async-done(((bf16[8,512,128]{1,2,0:T(8,128)(2,1)}), bf16[8,512,128]{1,2,0:T(8,128)(2,1)S(1)}, u32[]{:S(2)}, u32[]{:S(2)}) %all-to-all-start) | async-done | bytes 1048608 | tf_op jit(solution)/shard_map/all_to_all | solution.py:222
  620.2 123.5 %all-gather.7.cloned.1.call-done = bf16[4096,1024]{1,0:T(8,128)(2,1)} async-done(((bf16[512,1024]{1,0:T(8,128)(2,1)}), bf16[4096,1024]{1,0:T(8,128)(2,1)}) %all-gather.7.cloned.1.call-update) | async-done | bytes 8388624 | tf_op jit(solution)/shard_map/all_gather | solution.py:229
  743.6 10.0 multiply_convert_fusion.3
  755.6 6.7 convolution_convert_fusion.1
  763.1 145.0 %reduce-scatter.5.cloned.1.call-done = bf16[512,1024]{1,0:T(8,128)(2,1)} async-done(((bf16[4096,1024]{1,0:T(8,128)(2,1)}), bf16[512,1024]{1,0:T(8,128)(2,1)}) %reduce-scatter.5.cloned.1.call-update) | async-done | bytes 1048592 | tf_op jit(solution)/shard_map/reduce_scatter | solution.py:233
  917.4 123.6 %all-gather.9.cloned.1.call-done = bf16[4096,1024]{1,0:T(8,128)(2,1)} async-done(((bf16[512,1024]{1,0:T(8,128)(2,1)}), bf16[4096,1024]{1,0:T(8,128)(2,1)}) %all-gather.9.cloned.1.call-update) | async-done | bytes 8388624 | tf_op jit(solution)/shard_map/all_gather | solution.py:265
  1041.0 12.5 fusion.209
  1055.5 7.2 convolution_convert_fusion
  1086.0 8.1 fusion.123
  1094.1 114.5 %reduce-scatter.7.cloned.1.call-done = bf16[512,1024]{1,0:T(8,128)(2,1)} async-done(((bf16[4096,1024]{1,0:T(8,128)(2,1)}), bf16[512,1024]{1,0:T(8,128)(2,1)}) %reduce-scatter.7.cloned.1.call-update) | async-done | bytes 1048592 | tf_op jit(solution)/shard_map/reduce_scatter | solution.py:281
  1225.6 10.3 convolution_convert_fusion.3
  1235.9 8.2 convolution_convert_fusion.4
  1281.5 8.0 multiply_reduce_fusion.1
  1289.8 7.1 fusion.44
  1298.6 9.3 multiply_convert_fusion.1
  1319.5 11.4 multiply_reduce_fusion
  1330.9 7.9 fusion.55
  1349.7 12.4 multiply_convert_fusion
  1382.4 7.0 fusion.96
  1389.5 8.8 bitcast_convert_fusion
  1408.5 48.6 %all-reduce.11.cloned.1.call-done = (bf16[3,1024,128]{1,2,0:T(8,128)(2,1)}, bf16[128,1024]{1,0:T(8,128)(2,1)}, bf16[1024,512]{1,0:T(8,128)(2,1)}, bf16[512,1024]{1,0:T(8,128)(2,1)}) async-done(((bf16[3,1024,128]{1,2,0:T(8,128)(2,1)}, bf16[128,1024]{1,0:T(8,128)(2,1)}, bf16[1024,512]{1,0:T(8,128)(2,1)}, bf16[512,1024]{1,0:T(8,128)(2,1)}), (bf16[3,1024,128]{1,2,0:T(8,128)(2,1)}, bf16[128,1024]{1,0:T(8,128)(2,1)}, ...) | async-done | bytes 3145744 | tf_op jit(solution)/shard_map/psum | solution.py:354
  1466.1 142.2 %reduce-scatter.9.cloned.1.call-done = bf16[512,1024]{1,0:T(8,128)(2,1)} async-done(((bf16[4096,1024]{1,0:T(8,128)(2,1)}), bf16[512,1024]{1,0:T(8,128)(2,1)}) %reduce-scatter.9.cloned.1.call-update) | async-done | bytes 1048592 | tf_op jit(solution)/shard_map/reduce_scatter | solution.py:324
  1610.7 40.3 %all-reduce.6 = (f32[1024]{0:T(1024)}, f32[1024]{0:T(1024)}, f32[4,1024]{1,0:T(4,128)}, f32[4,1024]{1,0:T(4,128)}) all-reduce(f32[1024]{0:T(1024)S(1)} %copy-done.82, f32[1024]{0:T(1024)S(1)} %copy-done.78, f32[4,1024]{1,0:T(4,128)S(1)} %pad_maximum_fusion.15, ...), channel_id=1, replica_groups=mesh['wide'=4,'narrow'=8] {'wide','narrow'}, use_global_device_ids=true, to_apply=%region_39.40 | all-reduce | flops 10240 | bytes 81920 | tf_op jit(solution)/shard_map/psum | solution.py:361
  (378 shorter events, 348.1 us)
Async XLA Ops:
  7.2 736.5 %copy-start = (bf16[1024,512]{1,0:T(8,128)(2,1)S(1)}, bf16[1024,512]{1,0:T(8,128)(2,1)}, u32[]{:S(2)}) copy-start(bf16[1024,512]{1,0:T(8,128)(2,1)} %param.22) | copy-start | bytes 3145732
  7.2 464.4 %all-gather.11.cloned.1.call-start = ((), (), s32[]{:S(2)}) async-start(), calls=%async_computation.11 | async-start | bytes 9437184 | tf_op jit(solution)/shard_map/all_gather | solution.py:293
  16.4 569.3 %all-gather.5.cloned.1.call-start = ((), (), s32[]{:S(2)}) async-start(), calls=%async_computation.6 | async-start | bytes 2359296 | tf_op jit(solution)/shard_map/all_gather | solution.py:223
  16.5 46.7 %collective-permute-start = (bf16[512,1024]{1,0:T(8,128)(2,1)}, bf16[512,1024]{1,0:T(8,128)(2,1)S(1)}, u32[]{:S(2)}, u32[]{:S(2)}) collective-permute-start(bf16[512,1024]{1,0:T(8,128)(2,1)} %get-tuple-element.94), channel_id=1, source_target_pairs={{0,7},{1,0},{2,1},{3,2},{4,3},{5,4},{6,5},{7,6},{8,15},{9,8},{10,9... | collective-permute-start | bytes 3145736 | tf_op jit(solution)/shard_map/ppermute | solution.py:22
  65.0 58.8 %collective-permute-start.1 = (bf16[1024,1024]{1,0:T(8,128)(2,1)S(1)}, bf16[1024,1024]{1,0:T(8,128)(2,1)S(1)}, u32[]{:S(2)}, u32[]{:S(2)}) collective-permute-start(bf16[1024,1024]{1,0:T(8,128)(2,1)S(1)} %pad_maximum_fusion.1), channel_id=1, source_target_pairs={{0,6},{1,7},{2,0},{3,1},{4,2},{5,3},{6,4},{7,5},{8,14},{9,15},{10,... | collective-permute-start | bytes 6291464 | tf_op jit(solution)/shard_map/ppermute | solution.py:22
  127.5 258.2 %collective-permute-start.2 = (bf16[2048,1024]{1,0:T(8,128)(2,1)}, bf16[2048,1024]{1,0:T(8,128)(2,1)}, u32[]{:S(2)}, u32[]{:S(2)}) collective-permute-start(bf16[2048,1024]{1,0:T(8,128)(2,1)} %pad_maximum_fusion), channel_id=1, source_target_pairs={{0,4},{1,5},{2,6},{3,7},{4,0},{5,1},{6,2},{7,3},{8,12},{9,13},{10,... | collective-permute-start | bytes 12582920 | tf_op jit(solution)/shard_map/ppermute | solution.py:22
  134.3 440.5 %copy-start.18 = (pred[512,2048]{1,0:T(8,128)(4,1)}, pred[512,2048]{1,0:T(8,128)(4,1)S(1)}, u32[]{:S(2)}) copy-start(pred[512,2048]{1,0:T(8,128)(4,1)S(1)} %iota_compare_fusion) | copy-start | bytes 3145732
  138.4 253.0 %copy-start.27 = (bf16[512,1024]{1,0:T(8,128)(2,1)S(1)}, bf16[512,1024]{1,0:T(8,128)(2,1)}, u32[]{:S(2)}) copy-start(bf16[512,1024]{1,0:T(8,128)(2,1)} %copy-done.26) | copy-start | bytes 3145732
  582.1 28.7 %all-to-all-start = ((bf16[8,512,128]{1,2,0:T(8,128)(2,1)}), bf16[8,512,128]{1,2,0:T(8,128)(2,1)S(1)}, u32[]{:S(2)}, u32[]{:S(2)}) async-start(bf16[8,512,128]{1,2,0:T(8,128)(2,1)} %copy.144), calls=%async_computation | async-start | bytes 2097152 | tf_op jit(solution)/shard_map/all_to_all | solution.py:222
  585.7 158.0 %all-gather.7.cloned.1.call-start = ((), (), s32[]{:S(2)}) async-start(), calls=%async_computation.7 | async-start | bytes 9437184 | tf_op jit(solution)/shard_map/all_gather | solution.py:229
  617.4 126.2 %copy-start.93 = (f32[512]{0:T(512)S(1)}, f32[512]{0:T(512)}, u32[]{:S(2)}) copy-start(f32[512]{0:T(512)} %param.23) | copy-start | bytes 6148
  620.1 288.0 %reduce-scatter.5.cloned.1.call-start = ((), (), s32[]{:S(2)}) async-start(), calls=%async_computation.8 | async-start | bytes 9437184 | tf_op jit(solution)/shard_map/reduce_scatter | solution.py:233
  762.3 145.9 %copy-start.67 = (f32[1024]{0:T(1024)S(1)}, f32[1024]{0:T(1024)}, u32[]{:S(2)}) copy-start(f32[1024]{0:T(1024)} %param.25) | copy-start | bytes 12292
  762.3 149.2 %copy-start.72 = (f32[1,1024]{1,0:T(1,128)S(1)}, f32[1,1024]{1,0:T(1,128)}, u32[]{:S(2)}) copy-start(f32[1,1024]{1,0:T(1,128)} %get-tuple-element.132) | copy-start | bytes 12292
  762.3 278.7 %all-gather.9.cloned.1.call-start = ((), (), s32[]{:S(2)}) async-start(), calls=%async_computation.9 | async-start | bytes 9437184 | tf_op jit(solution)/shard_map/all_gather | solution.py:265
  917.3 291.2 %reduce-scatter.7.cloned.1.call-start = ((), (), s32[]{:S(2)}) async-start(), calls=%async_computation.10 | async-start | bytes 9437184 | tf_op jit(solution)/shard_map/reduce_scatter | solution.py:281
  1221.9 29.6 %all-to-all-start.1 = ((bf16[512,8,128]{0,2,1:T(8,128)(2,1)}), bf16[512,8,128]{0,2,1:T(8,128)(2,1)S(1)}, u32[]{:S(2)}, u32[]{:S(2)}) async-start(bf16[512,8,128]{0,2,1:T(8,128)(2,1)} %bitcast.18), calls=%async_computation.3 | async-start | bytes 2097152 | tf_op jit(solution)/shard_map/all_to_all | solution.py:300
  1225.5 163.9 %reduce-scatter.11.cloned.1.call-start = ((), (), s32[]{:S(2)}) async-start(), calls=%async_computation.13 | async-start | bytes 2359296 | tf_op jit(solution)/shard_map/reduce_scatter | solution.py:308
  1246.7 210.4 %all-reduce.11.cloned.1.call-start = ((), (), s32[]{:S(2)}) async-start(), calls=%async_computation.14 | async-start | bytes 6291456 | tf_op jit(solution)/shard_map/psum | solution.py:354
  1389.4 218.8 %reduce-scatter.9.cloned.1.call-start = ((), (), s32[]{:S(2)}) async-start(), calls=%async_computation.12 | async-start | bytes 9437184 | tf_op jit(solution)/shard_map/reduce_scatter | solution.py:324
  1459.0 149.3 %copy-start.7 = (bf16[512,1024]{1,0:T(8,128)(2,1)S(1)}, bf16[512,1024]{1,0:T(8,128)(2,1)}, u32[]{:S(2)}) copy-start(bf16[512,1024]{1,0:T(8,128)(2,1)} %param.14) | copy-start | bytes 3145732
  1459.0 149.3 %copy-start.71 = (f32[1,1024]{1,0:T(1,128)S(1)}, f32[1,1024]{1,0:T(1,128)}, u32[]{:S(2)}) copy-start(f32[1,1024]{1,0:T(1,128)} %copy-done.70) | copy-start | bytes 12292
  1459.0 149.3 %copy-start.74 = (f32[512]{0:T(512)S(1)}, f32[512]{0:T(512)}, u32[]{:S(2)}) copy-start(f32[512]{0:T(512)} %copy-done.73) | copy-start | bytes 6148
  1459.0 149.3 %copy-start.76 = (f32[512]{0:T(512)S(1)}, f32[512]{0:T(512)}, u32[]{:S(2)}) copy-start(f32[512]{0:T(512)} %copy-done.75) | copy-start | bytes 6148
  1461.6 148.9 %copy-start.80 = (f32[1024]{0:T(1024)S(1)}, f32[1024]{0:T(1024)}, u32[]{:S(2)}) copy-start(f32[1024]{0:T(1024)} %get-tuple-element.64) | copy-start | bytes 12292
  1461.6 149.0 %copy-start.81 = (f32[1024]{0:T(1024)S(1)}, f32[1024]{0:T(1024)}, u32[]{:S(2)}) copy-start(f32[1024]{0:T(1024)} %get-tuple-element.60) | copy-start | bytes 12292
  1461.6 149.0 %copy-start.85 = (f32[1024]{0:T(1024)S(1)}, f32[1024]{0:T(1024)}, u32[]{:S(2)}) copy-start(f32[1024]{0:T(1024)} %get-tuple-element.62) | copy-start | bytes 12292
  1461.6 149.0 %copy-start.79 = (f32[1024]{0:T(1024)S(1)}, f32[1024]{0:T(1024)}, u32[]{:S(2)}) copy-start(f32[1024]{0:T(1024)} %get-tuple-element.73) | copy-start | bytes 12292
  1461.6 149.0 %copy-start.84 = (f32[1024]{0:T(1024)S(1)}, f32[1024]{0:T(1024)}, u32[]{:S(2)}) copy-start(f32[1024]{0:T(1024)} %get-tuple-element.75) | copy-start | bytes 12292
  1461.6 149.0 %copy-start.78 = (f32[1024]{0:T(1024)S(1)}, f32[1024]{0:T(1024)}, u32[]{:S(2)}) copy-start(f32[1024]{0:T(1024)} %get-tuple-element.86) | copy-start | bytes 12292
  1461.6 149.0 %copy-start.82 = (f32[1024]{0:T(1024)S(1)}, f32[1024]{0:T(1024)}, u32[]{:S(2)}) copy-start(f32[1024]{0:T(1024)} %get-tuple-element.88) | copy-start | bytes 12292
  1464.5 190.1 %copy-start.1 = (bf16[1024,512]{1,0:T(8,128)(2,1)S(1)}, bf16[1024,512]{1,0:T(8,128)(2,1)}, u32[]{:S(2)}) copy-start(bf16[1024,512]{1,0:T(8,128)(2,1)} %param.22) | copy-start | bytes 3145732
  (85 other events, 779.2 us)
Sparse Core Ops, SparseCore 0:
  16.5 306.6 all-gather.10
  325.3 85.9 all-gather.4
  620.2 123.3 all-gather.6
  762.5 145.6 reduce-scatter.4
  917.5 123.5 all-gather.8
  1062.8 145.6 reduce-scatter.6
  1246.8 69.7 reduce-scatter.10
  1389.6 67.4 all-reduce.10
  1460.7 147.5 reduce-scatter.8
